TPU v7x, 256 devices: a whole 4x4x8 slice. The times are simulated.
256 devices in a mesh: row: 8 (over x, core), col: 32 (over z, y).
Axes of the slice: x: 4, y: 4, z: 8, core: 2. Of those that a mesh axis runs over, the one named last changes fastest.
Arguments:
- row_points: bfloat16 [512, 64, 256], P('row'), may hold values from -25.5 to 25.5
- col_points: bfloat16 [128, 64, 256], P('col'), may hold values from -25.5 to 25.5
- block_lists: int32 [512, 16], P('row'), may hold values from 0 to 127, as said below
Outputs:
- row_potential: float32 [512, 256], P('row')
- col_potential: float32 [128, 256], P('col')
Inputs may be any that keep to these rules, and one draw needn't show every extreme that they name: `block_lists`: the 16 column blocks of a row block are distinct. Among the row blocks of one index of row, at most 64 list entries name column blocks of one index of col, and exactly 64 for some index of col. Every column block is named by some row block of every index of row.
All inputs are finite; a program needn't handle non-finite values.
Results may differ from a plain program's by a relative error of at most 0.0003.
Values sent between devices are 32-bit elements; how exact they have to be, the bound alone decides.
No kernel may reach another device: no remote copies, remote signals or barrier semaphores. Data moves between devices by JAX's collectives and lax.ppermute only.
A program may use at most 64 MiB of HBM per device.

v0:
```python
import math
import jax
import jax.numpy as jnp
from jax import lax
from jax.sharding import PartitionSpec as P

DIM = 64
ITERS = 4
CAPACITY = 64
eps_reg = 0.05
neg_big = -1e30
group_slots = 8


def tile_partials(
    row_points, col_points, row_norms, col_norms, row_index, col_index, biases, over_columns
):
    row_tiles = row_points[row_index]
    col_tiles = col_points[col_index]
    inner_prod = jnp.einsum(
        "sdp,sdq->spq", row_tiles, col_tiles, preferred_element_type=jnp.float32
    )
    cost_tile = (
        row_norms[row_index][:, :, None] + col_norms[col_index][:, None, :] - 2.0 * inner_prod
    ) / DIM
    if over_columns:
        scores = (biases[:, None, :] - cost_tile) / eps_reg
        reduce_axis = 2
    else:
        scores = (biases[:, :, None] - cost_tile) / eps_reg
        reduce_axis = 1
    peak_vals = jnp.max(scores, axis=reduce_axis)
    totals = jnp.sum(jnp.exp(scores - jnp.expand_dims(peak_vals, reduce_axis)), axis=reduce_axis)
    return (peak_vals, totals)


def slot_partials(
    row_points, col_points, row_norms, col_norms, row_slot, col_slot, biases, over_columns
):
    groups = row_slot.shape[0] // group_slots
    block_size = row_points.shape[2]

    def one_group(members):
        return tile_partials(
            row_points,
            col_points,
            row_norms,
            col_norms,
            members[0],
            members[1],
            members[2],
            over_columns,
        )

    peak_parts, sum_parts = lax.map(
        one_group,
        (
            row_slot.reshape(groups, group_slots),
            col_slot.reshape(groups, group_slots),
            biases.reshape(groups, group_slots, block_size),
        ),
    )
    return (peak_parts.reshape(-1, block_size), sum_parts.reshape(-1, block_size))


def block_combine(peak_parts, sum_parts, members, slot_block, usable):
    block_peak = jnp.max(jnp.where(members[:, :, None], peak_parts[None, :, :], neg_big), axis=1)
    scale = jnp.where(usable[:, None], jnp.exp(peak_parts - block_peak[slot_block]), 0.0)
    block_sum = jnp.dot(
        members.astype(jnp.float32), sum_parts * scale, precision=lax.Precision.HIGHEST
    )
    return (block_peak, block_sum)


def potential_from(peak_vals, totals, log_mass):
    return eps_reg * (log_mass - (peak_vals + jnp.log(totals)))


def body(row_points, col_points, block_lists):
    row_blocks_here = row_points.shape[0]
    col_blocks_here = col_points.shape[0]
    block_size = row_points.shape[2]
    row_mass = -math.log(lax.axis_size("row") * row_blocks_here * block_size)
    col_mass = -math.log(lax.axis_size("col") * col_blocks_here * block_size)
    row_norms = jnp.sum(jnp.square(row_points.astype(jnp.float32)), axis=1)
    col_norms = jnp.sum(jnp.square(col_points.astype(jnp.float32)), axis=1)
    owned = (block_lists // col_blocks_here == lax.axis_index("col")).reshape(-1)
    entry_rank = jnp.cumsum(owned.astype(jnp.int32)) - 1
    slot_list = jnp.arange(CAPACITY, dtype=jnp.int32)
    picked = owned[None, :] & (entry_rank[None, :] == slot_list[:, None])
    entries = jnp.arange(owned.shape[0], dtype=jnp.int32)
    entry_of_slot = jnp.sum(jnp.where(picked, entries[None, :], 0), axis=1)
    usable = jnp.any(picked, axis=1)
    row_slot = entry_of_slot // block_lists.shape[1]
    col_slot = block_lists.reshape(-1)[entry_of_slot] % col_blocks_here
    row_members = (row_slot[None, :] == jnp.arange(row_blocks_here)[:, None]) & usable[None, :]
    col_members = (col_slot[None, :] == jnp.arange(col_blocks_here)[:, None]) & usable[None, :]
    col_potential = jnp.zeros((col_blocks_here, block_size), jnp.float32)
    row_potential = jnp.zeros((row_blocks_here, block_size), jnp.float32)
    for sweep in range(ITERS):
        peak_parts, sum_parts = slot_partials(
            row_points,
            col_points,
            row_norms,
            col_norms,
            row_slot,
            col_slot,
            col_potential[col_slot],
            True,
        )
        block_peak, block_sum = block_combine(peak_parts, sum_parts, row_members, row_slot, usable)
        whole_peak = lax.pmax(block_peak, "col")
        whole_sum = lax.psum(block_sum * jnp.exp(block_peak - whole_peak), "col")
        row_potential = potential_from(whole_peak, whole_sum, row_mass)
        peak_parts, sum_parts = slot_partials(
            row_points,
            col_points,
            row_norms,
            col_norms,
            row_slot,
            col_slot,
            row_potential[row_slot],
            False,
        )
        block_peak, block_sum = block_combine(peak_parts, sum_parts, col_members, col_slot, usable)
        whole_peak = lax.pmax(block_peak, "row")
        whole_sum = lax.psum(block_sum * jnp.exp(block_peak - whole_peak), "row")
        col_potential = potential_from(whole_peak, whole_sum, col_mass)
    return (row_potential, col_potential)


def solution(mesh):
    placed = (P("row", None, None), P("col", None, None), P("row", None))
    return jax.shard_map(
        body,
        mesh=mesh,
        in_specs=placed,
        out_specs=(P("row", None), P("col", None)),
        check_vma=False,
    )
```

profile of v0, /device:TPU:1, one launch (start us, length us, event | category | flops | bytes accessed | tf_op | source)
XLA Modules:
  0.0 1535.6 jit_solution(2969120463154943220)
XLA Ops:
  11.2 2.3 multiply_reduce_fusion
  14.2 32.7 %while.96 = (s32[]{:T(128)}, f32[8,8,256]{2,1,0:T(8,128)S(1)}, f32[8,8,256]{2,1,0:T(8,128)S(1)}, f32[8,8,256]{2,1,0:T(8,128)S(1)}, s32[8,8]{1,0:T(8,128)S(1)}, /...) while((s32[]{:T(128)}, f32[8,8,256]{2,1,0:T(8,128)S(1)}, ...), condition=%wide.region_9.10_spmd, body=%wide.region_6.9_spmd.sunk | while | flops 71825456 | bytes 5906877 | solution.py:55
  46.9 1.8 select_reduce_fusion.3
  50.3 139.6 %all-reduce.9.cloned.1.call-done = f32[64,256]{1,0:T(8,128)} async-done(((f32[64,256]{1,0:T(8,128)}), f32[64,256]{1,0:T(8,128)}) %all-reduce.9.cloned.1.call-update) | async-done | bytes 65552 | tf_op jit(solution)/shard_map/pmax | solution.py:112
  189.9 1.7 convolution_multiply_fusion.3
  191.7 141.8 %all-reduce.11.cloned.1.call-done = f32[64,256]{1,0:T(8,128)} async-done(((f32[64,256]{1,0:T(8,128)}), f32[64,256]{1,0:T(8,128)}) %all-reduce.11.cloned.1.call-update) | async-done | bytes 65552 | tf_op jit(solution)/shard_map/psum | solution.py:113
  335.1 32.8 %while.97 = (s32[]{:T(128)}, f32[8,8,256]{2,1,0:T(8,128)S(1)}, f32[8,8,256]{2,1,0:T(8,128)S(1)}, f32[8,8,256]{2,1,0:T(8,128)S(1)}, s32[8,8]{1,0:T(8,128)S(1)}, /...) while((s32[]{:T(128)}, f32[8,8,256]{2,1,0:T(8,128)S(1)}, ...), condition=%wide.region_16.17_spmd, body=%wide.region_13.16_spmd.sunk | while | flops 71825456 | bytes 5906877 | solution.py:55
  368.8 16.7 %pmax.57 = f32[4,256]{1,0:T(4,128)S(1)} all-reduce(f32[4,256]{1,0:T(4,128)S(1)} %select_reduce_fusion.7), channel_id=1, replica_groups=mesh['row'=8,'col'=32] {'row'}, use_global_device_ids=true, to_apply=%region_18.19 | all-reduce | flops 1024 | bytes 8192 | tf_op jit(solution)/shard_map/pmax | solution.py:126
  385.7 12.4 psum.57
  398.8 32.8 %while.98 = (s32[]{:T(128)}, f32[8,8,256]{2,1,0:T(8,128)S(1)}, f32[8,8,256]{2,1,0:T(8,128)S(1)}, f32[8,8,256]{2,1,0:T(8,128)S(1)}, s32[8,8]{1,0:T(8,128)S(1)}, /...) while((s32[]{:T(128)}, f32[8,8,256]{2,1,0:T(8,128)S(1)}, ...), condition=%wide.region_23.24_spmd, body=%wide.region_20.23_spmd.sunk | while | flops 71825456 | bytes 5906877 | solution.py:55
  431.6 1.8 select_reduce_fusion.2
  435.0 131.6 %all-reduce.13.cloned.1.call-done = f32[64,256]{1,0:T(8,128)} async-done(((f32[64,256]{1,0:T(8,128)}), f32[64,256]{1,0:T(8,128)}) %all-reduce.13.cloned.1.call-update) | async-done | bytes 65552 | tf_op jit(solution)/shard_map/pmax | solution.py:112
  568.5 141.7 %all-reduce.15.cloned.1.call-done = f32[64,256]{1,0:T(8,128)} async-done(((f32[64,256]{1,0:T(8,128)}), f32[64,256]{1,0:T(8,128)}) %all-reduce.15.cloned.1.call-update) | async-done | bytes 65552 | tf_op jit(solution)/shard_map/psum | solution.py:113
  711.7 32.8 %while.99 = (s32[]{:T(128)}, f32[8,8,256]{2,1,0:T(8,128)S(1)}, f32[8,8,256]{2,1,0:T(8,128)S(1)}, f32[8,8,256]{2,1,0:T(8,128)S(1)}, s32[8,8]{1,0:T(8,128)S(1)}, /...) while((s32[]{:T(128)}, f32[8,8,256]{2,1,0:T(8,128)S(1)}, ...), condition=%wide.region_30.31_spmd, body=%wide.region_27.30_spmd.sunk | while | flops 71825456 | bytes 5906877 | solution.py:55
  745.4 16.7 %pmax.59 = f32[4,256]{1,0:T(4,128)S(1)} all-reduce(f32[4,256]{1,0:T(4,128)S(1)} %select_reduce_fusion.6), channel_id=1, replica_groups=mesh['row'=8,'col'=32] {'row'}, use_global_device_ids=true, to_apply=%region_32.33 | all-reduce | flops 1024 | bytes 8192 | tf_op jit(solution)/shard_map/pmax | solution.py:126
  762.3 12.4 psum.59
  775.4 32.8 %while.100 = (s32[]{:T(128)}, f32[8,8,256]{2,1,0:T(8,128)S(1)}, f32[8,8,256]{2,1,0:T(8,128)S(1)}, f32[8,8,256]{2,1,0:T(8,128)S(1)}, s32[8,8]{1,0:T(8,128)S(1)}, ...) while((s32[]{:T(128)}, f32[8,8,256]{2,1,0:T(8,128)S(1)}, ...), condition=%wide.region_37.38_spmd, body=%wide.region_34.37_spmd.sunk | while | flops 71825456 | bytes 5906877 | solution.py:55
  808.2 1.8 select_reduce_fusion.1
  811.6 131.6 %all-reduce.17.cloned.1.call-done = f32[64,256]{1,0:T(8,128)} async-done(((f32[64,256]{1,0:T(8,128)}), f32[64,256]{1,0:T(8,128)}) %all-reduce.17.cloned.1.call-update) | async-done | bytes 65552 | tf_op jit(solution)/shard_map/pmax | solution.py:112
  943.2 1.7 convolution_multiply_fusion.1
  945.1 141.7 %all-reduce.19.cloned.1.call-done = f32[64,256]{1,0:T(8,128)} async-done(((f32[64,256]{1,0:T(8,128)}), f32[64,256]{1,0:T(8,128)}) %all-reduce.19.cloned.1.call-update) | async-done | bytes 65552 | tf_op jit(solution)/shard_map/psum | solution.py:113
  1088.3 32.8 %while.101 = (s32[]{:T(128)}, f32[8,8,256]{2,1,0:T(8,128)S(1)}, f32[8,8,256]{2,1,0:T(8,128)S(1)}, f32[8,8,256]{2,1,0:T(8,128)S(1)}, s32[8,8]{1,0:T(8,128)S(1)}, ...) while((s32[]{:T(128)}, f32[8,8,256]{2,1,0:T(8,128)S(1)}, ...), condition=%wide.region_44.45_spmd, body=%wide.region_41.44_spmd.sunk | while | flops 71825456 | bytes 5906877 | solution.py:55
  1122.0 16.7 %pmax.61 = f32[4,256]{1,0:T(4,128)S(1)} all-reduce(f32[4,256]{1,0:T(4,128)S(1)} %select_reduce_fusion.5), channel_id=1, replica_groups=mesh['row'=8,'col'=32] {'row'}, use_global_device_ids=true, to_apply=%region_46.47 | all-reduce | flops 1024 | bytes 8192 | tf_op jit(solution)/shard_map/pmax | solution.py:126
  1138.9 12.6 psum.61
  1152.2 32.8 %while.102 = (s32[]{:T(128)}, f32[8,8,256]{2,1,0:T(8,128)S(1)}, f32[8,8,256]{2,1,0:T(8,128)S(1)}, f32[8,8,256]{2,1,0:T(8,128)S(1)}, s32[8,8]{1,0:T(8,128)S(1)}, ...) while((s32[]{:T(128)}, f32[8,8,256]{2,1,0:T(8,128)S(1)}, ...), condition=%wide.region_51.52_spmd, body=%wide.region_48.51_spmd.sunk | while | flops 71825456 | bytes 5906877 | solution.py:55
  1185.0 1.8 select_reduce_fusion
  1188.4 131.6 %all-reduce.21.cloned.1.call-done = f32[64,256]{1,0:T(8,128)} async-done(((f32[64,256]{1,0:T(8,128)}), f32[64,256]{1,0:T(8,128)}) %all-reduce.21.cloned.1.call-update) | async-done | bytes 65552 | tf_op jit(solution)/shard_map/pmax | solution.py:112
  1320.0 1.7 convolution_multiply_fusion
  1321.8 141.9 %all-reduce.23.cloned.1.call-done = f32[64,256]{1,0:T(8,128)} async-done(((f32[64,256]{1,0:T(8,128)}), f32[64,256]{1,0:T(8,128)}) %all-reduce.23.cloned.1.call-update) | async-done | bytes 65552 | tf_op jit(solution)/shard_map/psum | solution.py:113
  1465.3 32.7 %while.103 = (s32[]{:T(128)}, f32[8,8,256]{2,1,0:T(8,128)S(1)}, f32[8,8,256]{2,1,0:T(8,128)S(1)}, f32[8,8,256]{2,1,0:T(8,128)S(1)}, s32[8,8]{1,0:T(8,128)S(1)}, ...) while((s32[]{:T(128)}, f32[8,8,256]{2,1,0:T(8,128)S(1)}, ...), condition=%wide.region_58.59_spmd, body=%wide.region_55.58_spmd.sunk | while | flops 71825456 | bytes 5906877 | solution.py:55
  1498.7 16.8 %pmax.63 = f32[4,256]{1,0:T(4,128)S(1)} all-reduce(f32[4,256]{1,0:T(4,128)S(1)} %select_reduce_fusion.4), channel_id=1, replica_groups=mesh['row'=8,'col'=32] {'row'}, use_global_device_ids=true, to_apply=%region_60.61 | all-reduce | flops 1024 | bytes 8192 | tf_op jit(solution)/shard_map/pmax | solution.py:126
  1515.7 12.4 psum.63
  (868 shorter events, 282.0 us)
Async XLA Ops:
  7.2 7.0 copy-start.1
  7.2 6.3 copy-start
  7.2 182.7 %all-reduce.9.cloned.1.call-start = ((), (), s32[]{:S(2)}) async-start(), calls=%async_computation | async-start | bytes 131072 | tf_op jit(solution)/shard_map/pmax | solution.py:112
  48.8 284.8 %all-reduce.11.cloned.1.call-start = ((), (), s32[]{:S(2)}) async-start(), calls=%async_computation.1 | async-start | bytes 131072 | tf_op jit(solution)/shard_map/psum | solution.py:113
  191.7 375.0 %all-reduce.13.cloned.1.call-start = ((), (), s32[]{:S(2)}) async-start(), calls=%async_computation.2 | async-start | bytes 131072 | tf_op jit(solution)/shard_map/pmax | solution.py:112
  433.5 276.7 %all-reduce.15.cloned.1.call-start = ((), (), s32[]{:S(2)}) async-start(), calls=%async_computation.3 | async-start | bytes 131072 | tf_op jit(solution)/shard_map/psum | solution.py:113
  568.4 374.8 %all-reduce.17.cloned.1.call-start = ((), (), s32[]{:S(2)}) async-start(), calls=%async_computation.4 | async-start | bytes 131072 | tf_op jit(solution)/shard_map/pmax | solution.py:112
  810.1 276.7 %all-reduce.19.cloned.1.call-start = ((), (), s32[]{:S(2)}) async-start(), calls=%async_computation.5 | async-start | bytes 131072 | tf_op jit(solution)/shard_map/psum | solution.py:113
  945.0 375.0 %all-reduce.21.cloned.1.call-start = ((), (), s32[]{:S(2)}) async-start(), calls=%async_computation.6 | async-start | bytes 131072 | tf_op jit(solution)/shard_map/pmax | solution.py:112
  1186.8 276.8 %all-reduce.23.cloned.1.call-start = ((), (), s32[]{:S(2)}) async-start(), calls=%async_computation.7 | async-start | bytes 131072 | tf_op jit(solution)/shard_map/psum | solution.py:113
  1464.6 0.7 copy-start.2
Sparse Core Ops, SparseCore 0:
  48.9 140.9 all-reduce.8
  193.9 139.5 all-reduce.10
  433.6 132.9 all-reduce.12
  570.5 139.5 all-reduce.14
  810.2 132.9 all-reduce.16
  947.1 139.5 all-reduce.18
  1187.0 133.0 all-reduce.20
  1324.0 139.5 all-reduce.22
where the time goes:
time: 1540 us
  waiting for transfers between devices  1100 us (71%)
  local copies, waits for them, and re-layouts  162 us (11%)
  blocking collectives  117 us (8%)
  matrix products  97.4 us (6%)
  other arithmetic  37 us (2%)
    psum x4, waiting for transfers between devices, body(): whole_sum = lax.psum(block_sum * jnp.exp(block_peak - whole_peak), 'col')  567 us
    pmax x4, waiting for transfers between devices, body(): whole_peak = lax.pmax(block_peak, 'col')  534 us
    dot_general x64, matrix products, tile_partials(): jnp.einsum('sdp,sdq->spq', row_tiles, col_tiles, preferred_element_type=j...  89.7 us
    pmax x4, blocking collectives, body(): whole_peak = lax.pmax(block_peak, 'row')  67 us
    psum x4, blocking collectives, body(): whole_sum = lax.psum(block_sum * jnp.exp(block_peak - whole_peak), 'row')  49.8 us
    gather x64, local copies, waits for them, and re-layouts, tile_partials(): col_tiles = col_points[col_index]  36.1 us
    gather x64, local copies, waits for them, and re-layouts, tile_partials(): row_tiles = row_points[row_index]  36.1 us
    gather x64, local copies, waits for them, and re-layouts, tile_partials(): row_norms[row_index][:, :, None] + col_norms[col_index][:, None, :]  36 us
  transfers between devices with their start and end apart: 8, of which 8 were waited for; matrix products, arithmetic and copies ran while one was open for 0% of the time, Pallas kernels for 0%

commit v1 on v0

--- a/solution.py
+++ b/solution.py
@@ -10,6 +10,12 @@
 eps_reg = 0.05
 neg_big = -1e30
 group_slots = 8
+
+
+def gather_and_add(block, axis):
+    pieces = lax.all_gather(block, axis, axis=0, tiled=False)
+    acc = pieces.sum(axis=0)
+    return acc
 
 
 def tile_partials(
@@ -124,7 +130,7 @@
         )
         block_peak, block_sum = block_combine(peak_parts, sum_parts, col_members, col_slot, usable)
         whole_peak = lax.pmax(block_peak, "row")
-        whole_sum = lax.psum(block_sum * jnp.exp(block_peak - whole_peak), "row")
+        whole_sum = gather_and_add(block_sum * jnp.exp(block_peak - whole_peak), "row")
         col_potential = potential_from(whole_peak, whole_sum, col_mass)
     return (row_potential, col_potential)
 

time: 1540 us -> 1540 us (level)
    all_gather x0 -> x4, blocking collectives: none -> 53.6 us  [gather_and_add(): pieces = lax.all_gather(block, axis, axis=0, tiled=False)]
    psum x4 -> x0, blocking collectives: 49.8 us -> none  [body(): whole_sum = lax.psum(block_sum * jnp.exp(block_peak - whole_peak), 'row')]
where the time goes in v1:
time: 1540 us
  waiting for transfers between devices  1100 us (71%)
  local copies, waits for them, and re-layouts  162 us (11%)
  blocking collectives  121 us (8%)
  matrix products  97.5 us (6%)
  other arithmetic  37.1 us (2%)
    psum x4, waiting for transfers between devices, body(): whole_sum = lax.psum(block_sum * jnp.exp(block_peak - whole_peak), 'col')  567 us
    pmax x4, waiting for transfers between devices, body(): whole_peak = lax.pmax(block_peak, 'col')  536 us
    dot_general x64, matrix products, tile_partials(): jnp.einsum('sdp,sdq->spq', row_tiles, col_tiles, preferred_element_type=j...  89.7 us
    pmax x4, blocking collectives, body(): whole_peak = lax.pmax(block_peak, 'row')  67 us
    all_gather x4, blocking collectives, gather_and_add(): pieces = lax.all_gather(block, axis, axis=0, tiled=False)  53.6 us
    gather x64, local copies, waits for them, and re-layouts, tile_partials(): row_tiles = row_points[row_index]  36.1 us
    gather x64, local copies, waits for them, and re-layouts, tile_partials(): col_tiles = col_points[col_index]  36.1 us
    gather x64, local copies, waits for them, and re-layouts, tile_partials(): col_norms[col_index][:, None, :]  36 us
  transfers between devices with their start and end apart: 8, of which 8 were waited for; matrix products, arithmetic and copies ran while one was open for 0% of the time, Pallas kernels for 0%

profile of v1, /device:TPU:1, one launch (start us, length us, event | category | flops | bytes accessed | tf_op | source)
XLA Modules:
  0.0 1540.6 jit_solution(5097595745943214700)
XLA Ops:
  11.2 2.3 multiply_reduce_fusion
  14.2 32.7 %while.96 = (s32[]{:T(128)}, f32[8,8,256]{2,1,0:T(8,128)S(1)}, f32[8,8,256]{2,1,0:T(8,128)S(1)}, f32[8,8,256]{2,1,0:T(8,128)S(1)}, s32[8,8]{1,0:T(8,128)S(1)}, /...) while((s32[]{:T(128)}, f32[8,8,256]{2,1,0:T(8,128)S(1)}, ...), condition=%wide.region_9.10_spmd, body=%wide.region_6.9_spmd.sunk | while | flops 71825456 | bytes 5906877 | solution.py:61
  46.9 1.8 select_reduce_fusion.3
  50.3 139.6 %all-reduce.9.cloned.1.call-done = f32[64,256]{1,0:T(8,128)} async-done(((f32[64,256]{1,0:T(8,128)}), f32[64,256]{1,0:T(8,128)}) %all-reduce.9.cloned.1.call-update) | async-done | bytes 65552 | tf_op jit(solution)/shard_map/pmax | solution.py:118
  189.9 1.7 convolution_multiply_fusion.3
  191.7 141.8 %all-reduce.11.cloned.1.call-done = f32[64,256]{1,0:T(8,128)} async-done(((f32[64,256]{1,0:T(8,128)}), f32[64,256]{1,0:T(8,128)}) %all-reduce.11.cloned.1.call-update) | async-done | bytes 65552 | tf_op jit(solution)/shard_map/psum | solution.py:119
  335.1 32.8 %while.97 = (s32[]{:T(128)}, f32[8,8,256]{2,1,0:T(8,128)S(1)}, f32[8,8,256]{2,1,0:T(8,128)S(1)}, f32[8,8,256]{2,1,0:T(8,128)S(1)}, s32[8,8]{1,0:T(8,128)S(1)}, /...) while((s32[]{:T(128)}, f32[8,8,256]{2,1,0:T(8,128)S(1)}, ...), condition=%wide.region_16.17_spmd, body=%wide.region_13.16_spmd.sunk | while | flops 71825456 | bytes 5906877 | solution.py:61
  368.8 16.7 %pmax.57 = f32[4,256]{1,0:T(4,128)S(1)} all-reduce(f32[4,256]{1,0:T(4,128)S(1)} %select_reduce_fusion.7), channel_id=1, replica_groups=mesh['row'=8,'col'=32] {'row'}, use_global_device_ids=true, to_apply=%region_18.19 | all-reduce | flops 1024 | bytes 8192 | tf_op jit(solution)/shard_map/pmax | solution.py:132
  385.7 13.4 all-gather.4
  399.8 32.8 %while.98 = (s32[]{:T(128)}, f32[8,8,256]{2,1,0:T(8,128)S(1)}, f32[8,8,256]{2,1,0:T(8,128)S(1)}, f32[8,8,256]{2,1,0:T(8,128)S(1)}, s32[8,8]{1,0:T(8,128)S(1)}, /...) while((s32[]{:T(128)}, f32[8,8,256]{2,1,0:T(8,128)S(1)}, ...), condition=%wide.region_23.24_spmd, body=%wide.region_20.23_spmd.sunk | while | flops 71825456 | bytes 5906877 | solution.py:61
  432.6 1.8 select_reduce_fusion.2
  436.0 132.0 %all-reduce.13.cloned.1.call-done = f32[64,256]{1,0:T(8,128)} async-done(((f32[64,256]{1,0:T(8,128)}), f32[64,256]{1,0:T(8,128)}) %all-reduce.13.cloned.1.call-update) | async-done | bytes 65552 | tf_op jit(solution)/shard_map/pmax | solution.py:118
  568.1 1.7 convolution_multiply_fusion.2
  569.9 141.7 %all-reduce.15.cloned.1.call-done = f32[64,256]{1,0:T(8,128)} async-done(((f32[64,256]{1,0:T(8,128)}), f32[64,256]{1,0:T(8,128)}) %all-reduce.15.cloned.1.call-update) | async-done | bytes 65552 | tf_op jit(solution)/shard_map/psum | solution.py:119
  713.2 32.8 %while.99 = (s32[]{:T(128)}, f32[8,8,256]{2,1,0:T(8,128)S(1)}, f32[8,8,256]{2,1,0:T(8,128)S(1)}, f32[8,8,256]{2,1,0:T(8,128)S(1)}, s32[8,8]{1,0:T(8,128)S(1)}, /...) while((s32[]{:T(128)}, f32[8,8,256]{2,1,0:T(8,128)S(1)}, ...), condition=%wide.region_30.31_spmd, body=%wide.region_27.30_spmd.sunk | while | flops 71825456 | bytes 5906877 | solution.py:61
  746.8 16.7 %pmax.59 = f32[4,256]{1,0:T(4,128)S(1)} all-reduce(f32[4,256]{1,0:T(4,128)S(1)} %select_reduce_fusion.6), channel_id=1, replica_groups=mesh['row'=8,'col'=32] {'row'}, use_global_device_ids=true, to_apply=%region_32.33 | all-reduce | flops 1024 | bytes 8192 | tf_op jit(solution)/shard_map/pmax | solution.py:132
  763.7 13.4 all-gather.5
  777.8 32.8 %while.100 = (s32[]{:T(128)}, f32[8,8,256]{2,1,0:T(8,128)S(1)}, f32[8,8,256]{2,1,0:T(8,128)S(1)}, f32[8,8,256]{2,1,0:T(8,128)S(1)}, s32[8,8]{1,0:T(8,128)S(1)}, ...) while((s32[]{:T(128)}, f32[8,8,256]{2,1,0:T(8,128)S(1)}, ...), condition=%wide.region_37.38_spmd, body=%wide.region_34.37_spmd.sunk | while | flops 71825456 | bytes 5906877 | solution.py:61
  810.6 1.8 select_reduce_fusion.1
  814.0 132.0 %all-reduce.17.cloned.1.call-done = f32[64,256]{1,0:T(8,128)} async-done(((f32[64,256]{1,0:T(8,128)}), f32[64,256]{1,0:T(8,128)}) %all-reduce.17.cloned.1.call-update) | async-done | bytes 65552 | tf_op jit(solution)/shard_map/pmax | solution.py:118
  946.0 1.7 convolution_multiply_fusion.1
  948.0 141.5 %all-reduce.19.cloned.1.call-done = f32[64,256]{1,0:T(8,128)} async-done(((f32[64,256]{1,0:T(8,128)}), f32[64,256]{1,0:T(8,128)}) %all-reduce.19.cloned.1.call-update) | async-done | bytes 65552 | tf_op jit(solution)/shard_map/psum | solution.py:119
  1091.1 32.8 %while.101 = (s32[]{:T(128)}, f32[8,8,256]{2,1,0:T(8,128)S(1)}, f32[8,8,256]{2,1,0:T(8,128)S(1)}, f32[8,8,256]{2,1,0:T(8,128)S(1)}, s32[8,8]{1,0:T(8,128)S(1)}, ...) while((s32[]{:T(128)}, f32[8,8,256]{2,1,0:T(8,128)S(1)}, ...), condition=%wide.region_44.45_spmd, body=%wide.region_41.44_spmd.sunk | while | flops 71825456 | bytes 5906877 | solution.py:61
  1124.8 16.7 %pmax.61 = f32[4,256]{1,0:T(4,128)S(1)} all-reduce(f32[4,256]{1,0:T(4,128)S(1)} %select_reduce_fusion.5), channel_id=1, replica_groups=mesh['row'=8,'col'=32] {'row'}, use_global_device_ids=true, to_apply=%region_46.47 | all-reduce | flops 1024 | bytes 8192 | tf_op jit(solution)/shard_map/pmax | solution.py:132
  1141.7 13.4 all-gather.6
  1155.8 32.8 %while.102 = (s32[]{:T(128)}, f32[8,8,256]{2,1,0:T(8,128)S(1)}, f32[8,8,256]{2,1,0:T(8,128)S(1)}, f32[8,8,256]{2,1,0:T(8,128)S(1)}, s32[8,8]{1,0:T(8,128)S(1)}, ...) while((s32[]{:T(128)}, f32[8,8,256]{2,1,0:T(8,128)S(1)}, ...), condition=%wide.region_51.52_spmd, body=%wide.region_48.51_spmd.sunk | while | flops 71825456 | bytes 5906877 | solution.py:61
  1188.6 1.8 select_reduce_fusion
  1192.0 132.0 %all-reduce.21.cloned.1.call-done = f32[64,256]{1,0:T(8,128)} async-done(((f32[64,256]{1,0:T(8,128)}), f32[64,256]{1,0:T(8,128)}) %all-reduce.21.cloned.1.call-update) | async-done | bytes 65552 | tf_op jit(solution)/shard_map/pmax | solution.py:118
  1325.8 141.9 %all-reduce.23.cloned.1.call-done = f32[64,256]{1,0:T(8,128)} async-done(((f32[64,256]{1,0:T(8,128)}), f32[64,256]{1,0:T(8,128)}) %all-reduce.23.cloned.1.call-update) | async-done | bytes 65552 | tf_op jit(solution)/shard_map/psum | solution.py:119
  1469.3 32.7 %while.103 = (s32[]{:T(128)}, f32[8,8,256]{2,1,0:T(8,128)S(1)}, f32[8,8,256]{2,1,0:T(8,128)S(1)}, f32[8,8,256]{2,1,0:T(8,128)S(1)}, s32[8,8]{1,0:T(8,128)S(1)}, ...) while((s32[]{:T(128)}, f32[8,8,256]{2,1,0:T(8,128)S(1)}, ...), condition=%wide.region_58.59_spmd, body=%wide.region_55.58_spmd.sunk | while | flops 71825456 | bytes 5906877 | solution.py:61
  1502.8 16.7 %pmax.63 = f32[4,256]{1,0:T(4,128)S(1)} all-reduce(f32[4,256]{1,0:T(4,128)S(1)} %select_reduce_fusion.4), channel_id=1, replica_groups=mesh['row'=8,'col'=32] {'row'}, use_global_device_ids=true, to_apply=%region_60.61 | all-reduce | flops 1024 | bytes 8192 | tf_op jit(solution)/shard_map/pmax | solution.py:132
  1519.7 13.4 all-gather.7
  (872 shorter events, 282.2 us)
Async XLA Ops:
  7.2 7.0 copy-start.1
  7.2 6.3 copy-start
  7.2 182.7 %all-reduce.9.cloned.1.call-start = ((), (), s32[]{:S(2)}) async-start(), calls=%async_computation | async-start | bytes 131072 | tf_op jit(solution)/shard_map/pmax | solution.py:118
  48.8 284.8 %all-reduce.11.cloned.1.call-start = ((), (), s32[]{:S(2)}) async-start(), calls=%async_computation.1 | async-start | bytes 131072 | tf_op jit(solution)/shard_map/psum | solution.py:119
  191.7 376.4 %all-reduce.13.cloned.1.call-start = ((), (), s32[]{:S(2)}) async-start(), calls=%async_computation.2 | async-start | bytes 131072 | tf_op jit(solution)/shard_map/pmax | solution.py:118
  434.5 277.1 %all-reduce.15.cloned.1.call-start = ((), (), s32[]{:S(2)}) async-start(), calls=%async_computation.3 | async-start | bytes 131072 | tf_op jit(solution)/shard_map/psum | solution.py:119
  569.8 376.2 %all-reduce.17.cloned.1.call-start = ((), (), s32[]{:S(2)}) async-start(), calls=%async_computation.4 | async-start | bytes 131072 | tf_op jit(solution)/shard_map/pmax | solution.py:118
  812.5 277.1 %all-reduce.19.cloned.1.call-start = ((), (), s32[]{:S(2)}) async-start(), calls=%async_computation.5 | async-start | bytes 131072 | tf_op jit(solution)/shard_map/psum | solution.py:119
  947.8 376.2 %all-reduce.21.cloned.1.call-start = ((), (), s32[]{:S(2)}) async-start(), calls=%async_computation.6 | async-start | bytes 131072 | tf_op jit(solution)/shard_map/pmax | solution.py:118
  1190.5 277.2 %all-reduce.23.cloned.1.call-start = ((), (), s32[]{:S(2)}) async-start(), calls=%async_computation.7 | async-start | bytes 131072 | tf_op jit(solution)/shard_map/psum | solution.py:119
  1468.6 0.7 copy-start.2
Sparse Core Ops, SparseCore 0:
  48.9 140.9 all-reduce.8
  193.9 139.5 all-reduce.10
  434.6 133.4 all-reduce.12
  571.9 139.5 all-reduce.14
  812.6 133.3 all-reduce.16
  949.9 139.5 all-reduce.18
  1190.6 133.4 all-reduce.20
  1328.1 139.5 all-reduce.22
